TPU v7x, 32 devices: a whole 2x2x4 slice. The times are simulated.
32 devices in a mesh: layer: 2 (over x), row: 4 (over y, core), col: 4 (over z).
Axes of the slice: x: 2, y: 2, z: 4, core: 2. Of those that a mesh axis runs over, the one named last changes fastest.
Arguments:
- left_matrix: bfloat16 [8192, 1024], P('row', ('layer', 'col')), may hold values from -6 to 6
- square_term: bfloat16 [1024, 1024], P(('layer', 'row'), 'col'), may hold values from -0.5 to 0.5
- block_pattern: int32 [64, 8], replicated, may hold values from 0 to 1, as said below
- keep_mask: int32 [64, 8], replicated, may hold values 0 or 1
Outputs:
- product: bfloat16 [8192, 1024], P('row', 'col')
Inputs may be any that keep to these rules, and one draw needn't show every extreme that they name: `block_pattern`: in each aligned group of 16 block rows, every block column holds 1 to 8 stored blocks; some group holds exactly 8.
All inputs are finite; a program needn't handle non-finite values.
Results may differ from a plain program's by a relative error of at most 0.0038.
Values may be sent and summed in bfloat16 or wider, within the bound.
No kernel may reach another device: no remote copies, remote signals or barrier semaphores. Data moves between devices by JAX's collectives and lax.ppermute only.
A program may use at most 64 MiB of HBM per device.

v0:
```python
import jax
import jax.numpy as jnp
from jax import lax
from jax.sharding import PartitionSpec as P

BLK = 128
GROUP = 16
CAP = 8


def slot_table(pattern):
    stored = (pattern > 0).astype(jnp.int32)
    rows = pattern.shape[0]
    groups = rows // GROUP
    grouped = stored.reshape(groups, GROUP, -1)
    slot = jnp.cumsum(grouped, axis=1) - 1
    group_base = (jnp.arange(groups, dtype=jnp.int32) * CAP)[:, None, None]
    slot = (slot + group_base).reshape(rows, -1)
    return (stored, slot)


def per_device(left_matrix, square_term, block_pattern, keep_mask):
    row_idx = lax.axis_index("row")
    col_idx = lax.axis_index("col")
    layer_idx = lax.axis_index("layer")
    row_count = lax.axis_size("row")
    col_count = lax.axis_size("col")
    rows_local = left_matrix.shape[0]
    row_blocks = rows_local // BLK
    inner_blocks = left_matrix.shape[1] // BLK
    inner_local = square_term.shape[0]
    cols_local = square_term.shape[1]
    col_blocks = cols_local // BLK
    slots = row_blocks // GROUP * CAP
    total_inner_blocks = block_pattern.shape[1]
    inner_start = (layer_idx * col_count + col_idx) * inner_blocks
    pattern_patch = lax.dynamic_slice(
        block_pattern, (row_idx * row_blocks, inner_start), (row_blocks, inner_blocks)
    )
    stored, slot = slot_table(pattern_patch)
    slot_ids = jnp.arange(slots, dtype=jnp.int32)
    hit = (stored[:, :, None] > 0) & (slot[:, :, None] == slot_ids[None, None, :])
    source_row = jnp.sum(
        jnp.where(hit, jnp.arange(row_blocks, dtype=jnp.int32)[:, None, None], 0), axis=0
    )
    blocks = left_matrix.reshape(row_blocks, BLK, inner_blocks, BLK).transpose(2, 0, 1, 3)
    flat_blocks = blocks.reshape(inner_blocks * row_blocks, BLK, BLK)
    take_idx = source_row + (jnp.arange(inner_blocks, dtype=jnp.int32) * row_blocks)[:, None]
    packed = jnp.take(flat_blocks, take_idx.reshape(-1), axis=0)
    packed = packed.reshape(inner_blocks, slots, BLK, BLK)
    gathered = lax.all_gather(packed, ("layer", "col"), axis=0, tiled=True)
    first_inner = (layer_idx * row_count + row_idx) * inner_local
    first_col = col_idx * cols_local
    inner_pos = first_inner + lax.broadcasted_iota(jnp.int32, (inner_local, cols_local), 0)
    col_pos = first_col + lax.broadcasted_iota(jnp.int32, (inner_local, cols_local), 1)
    unit = jnp.where(inner_pos == col_pos, jnp.float32(1.5), jnp.float32(0.0))
    right_factor = (unit - 0.5 * square_term.astype(jnp.float32)).astype(jnp.bfloat16)
    right_full = lax.all_gather(right_factor, ("layer", "row"), axis=0, tiled=True)
    panel_pattern = lax.dynamic_slice(
        block_pattern, (row_idx * row_blocks, 0), (row_blocks, total_inner_blocks)
    )
    p_stored, p_slot = slot_table(panel_pattern)
    gather_idx = jnp.arange(total_inner_blocks, dtype=jnp.int32)[None, :] * slots + jnp.clip(
        p_slot, 0, slots - 1
    )
    flat_packed = gathered.reshape(total_inner_blocks * slots, BLK, BLK)
    right_blocks = right_full.reshape(total_inner_blocks, BLK, cols_local)

    def chunk_sum(first, count):
        idx = lax.dynamic_slice_in_dim(gather_idx, first, count, axis=1)
        keep = lax.dynamic_slice_in_dim(p_stored, first, count, axis=1)
        dense = jnp.take(flat_packed, idx.reshape(-1), axis=0)
        dense = dense.reshape(row_blocks, count, BLK, BLK)
        dense = jnp.where(keep[:, :, None, None] > 0, dense, jnp.zeros_like(dense))
        rhs = lax.dynamic_slice_in_dim(right_blocks, first, count, axis=0)
        return jnp.einsum("ijab,jbc->iac", dense, rhs, preferred_element_type=jnp.float32)

    dense_bytes = row_blocks * total_inner_blocks * BLK * BLK * 2
    chunks = max(1, dense_bytes // (4 << 20))
    while total_inner_blocks % chunks:
        chunks += 1
    if chunks == 1:
        full_sum = chunk_sum(0, total_inner_blocks)
    else:
        per_chunk = total_inner_blocks // chunks

        def body(c, acc):
            return acc + chunk_sum(c * per_chunk, per_chunk)

        full_sum = lax.fori_loop(
            0, chunks, body, jnp.zeros((row_blocks, BLK, cols_local), jnp.float32)
        )
    full_sum = full_sum.reshape(rows_local, cols_local)
    keep_patch = lax.dynamic_slice(
        keep_mask, (row_idx * row_blocks, col_idx * col_blocks), (row_blocks, col_blocks)
    )
    keep_full = jnp.repeat(jnp.repeat(keep_patch, BLK, axis=0), BLK, axis=1)
    kept = jnp.where(keep_full > 0, full_sum, jnp.zeros_like(full_sum))
    return kept.astype(jnp.bfloat16)


def solution(mesh):
    return jax.shard_map(
        per_device,
        mesh=mesh,
        in_specs=(P("row", ("layer", "col")), P(("layer", "row"), "col"), P(), P()),
        out_specs=P("row", "col"),
        check_vma=False,
    )
```

profile of v0, /device:TPU:0, one launch (start us, length us, event | category | flops | bytes accessed | tf_op | source)
XLA Modules:
  0.0 81.9 jit_solution(10551937533751118428)
XLA Ops:
  6.5 0.0 copy-start
  6.5 0.0 all-gather.2.cloned.1.call-start
  6.5 0.8 %compare_bitcast_fusion = (pred[16]{0:T(512)(128)(4,1)S(1)}, s32[16,1]{0,1:T(1,128)S(1)}) fusion(s32[64,8]{0,1:T(8,128)} %param.6, s32[]{:T(128)S(6)} %select_n.84, s32[]{:T(128)S(6)} %select_n.87), kind=kLoop, calls=%fused_computation.29 | loop fusion | flops 48 | bytes 152 | tf_op jit(solution)/shard_map/gt | solution.py:42
  7.4 0.1 copy.39
  7.5 0.1 add_reduce_fusion
  7.6 0.1 select_reduce_fusion
  7.8 0.0 copy-done
  7.8 0.6 gather_fusion
  8.4 0.8 bitcast_select_fusion
  9.2 0.0 all-gather.2.cloned.1.call-update
  9.2 0.8 convert_compare_fusion
  10.0 0.1 copy.36
  10.1 0.1 min.15
  10.2 0.1 copy.37
  10.3 0.1 add.128
  10.3 0.1 compare_and_fusion
  10.4 0.1 copy.38
  10.5 0.1 copy.35
  10.6 0.8 dynamic-slice_compare_fusion.1
  11.4 0.1 broadcast_bitcast_fusion
  11.5 0.1 broadcast_in_dim.66
  11.6 0.6 copy.43
  12.3 0.9 %subtract_convert_fusion = bf16[128,256]{1,0:T(8,128)(2,1)S(1)} fusion(bf16[128,256]{1,0:T(8,128)(2,1)} %param.5, s32[256]{0:T(256)S(1)} %iota_add_fusion, s32[128]{0:T(128)S(1)} %iota_add_fusion.1), kind=kLoop, calls=%fused_computation.9 | loop fusion | flops 196608 | bytes 132608 | tf_op jit(solution)/shard_map/convert_element_type | solution.py:57
  13.2 12.6 %all_gather.7 = bf16[1024,256]{1,0:T(8,128)(2,1)S(1)} all-gather(bf16[128,256]{1,0:T(8,128)(2,1)S(1)} %subtract_convert_fusion), channel_id=1, replica_groups=mesh['layer'=2,'row'=4,'col'=4] {'layer','row'}, dimensions={0}, use_global_device_ids=true | all-gather | bytes 589824 | tf_op jit(solution)/shard_map/all_gather | solution.py:58
  25.8 36.2 %all-gather.2.cloned.1.call-done = bf16[8,8,128,128]{3,2,1,0:T(8,128)(2,1)} async-done(((bf16[1,8,128,128]{3,2,1,0:T(8,128)(2,1)}), bf16[8,8,128,128]{3,2,1,0:T(8,128)(2,1)}) %all-gather.2.cloned.1.call-update) | async-done | bytes 2097168 | tf_op jit(solution)/shard_map/all_gather | solution.py:51
  62.0 4.6 %gather_fusion.1 = bf16[128,128,128]{2,1,0:T(8,128)(2,1)} fusion(bf16[64,128,128]{2,1,0:T(8,128)(2,1)} %bitcast.42, s32[1024]{0:T(1024)S(1)} %pad_clamp_fusion), kind=kCustom, calls=%fused_computation.1 | custom fusion | bytes 8389120 | tf_op jit(solution)/shard_map/jit(_take)/gather | solution.py:72
  66.6 2.6 %select_bitcast_fusion = bf16[16,128,128,8]{2,1,3,0:T(8,128)(2,1)S(1)} fusion(bf16[16,8,128,128]{3,2,1,0:T(8,128)(2,1)} %bitcast.41, pred[16,8]{1,0:T(8,128)(4,1)S(1)} %copy.38, pred[16,8]{1,0:T(8,128)(4,1)S(1)} %copy.35), kind=kLoop, calls=%fused_computation.4 | loop fusion | flops 4194304 | bytes 8388864 | tf_op jit(solution)/shard_map/ijab,jbc->iac/dot_general | solution.py:76
  69.2 3.5 %copy.41 = bf16[16,128,128,8]{2,3,1,0:T(8,128)(2,1)S(1)} copy(bf16[16,128,128,8]{2,1,3,0:T(8,128)(2,1)S(1)} %select_bitcast_fusion) | data formatting | bytes 8388608 | tf_op jit(solution)/shard_map/ijab,jbc->iac/dot_general | solution.py:76
  72.7 2.3 %fusion.8 = bf16[2048,256]{1,0:T(8,128)(2,1)} fusion(pred[2048,256]{1,0:T(32,128)(4,1)S(1)} %copy.43, bf16[8,128,256]{2,1,0:T(8,128)(2,1)S(1)} %bitcast.45, bf16[2048,128,8]{1,2,0:T(8,128)(2,1)S(1)} %bitcast.43), kind=kOutput, calls=%fused_computation.7 | convolution fusion | flops 1074790400 | bytes 6291456 | tf_op jit(solution)/shard_map/ijab,jbc->iac/dot_general | solution.py:76
  (14 shorter events, 0.2 us)
Async XLA Ops:
  6.5 1.2 %copy-start = (bf16[2048,128]{1,0:T(8,128)(2,1)S(1)}, bf16[2048,128]{1,0:T(8,128)(2,1)}, u32[]{:S(2)}) copy-start(bf16[2048,128]{1,0:T(8,128)(2,1)} %param.4) | copy-start | bytes 1572868
  6.5 55.5 %all-gather.2.cloned.1.call-start = ((), (), s32[]{:S(2)}) async-start(), calls=%async_computation | async-start | bytes 2359296 | tf_op jit(solution)/shard_map/all_gather | solution.py:51
Sparse Core Ops, SparseCore 0:
  9.5 52.4 all-gather.1
where the time goes:
time: 82.1 us; the launch traced here: 81.9 us
  waiting for transfers between devices  36.2 us (44%)
  between operations  13.5 us (16%)
  blocking collectives  12.6 us (15%)
  local copies, waits for them, and re-layouts  10.2 us (12%)
  other arithmetic  7.08 us (9%)
  matrix products  2.27 us (3%)
    all_gather x1, waiting for transfers between devices, per_device(): gathered = lax.all_gather(packed, ('layer', 'col'), axis=0, tiled=True)  36.2 us
    all_gather x1, blocking collectives, per_device(): lax.all_gather(right_factor, ('layer', 'row'), axis=0, tiled=True)  12.6 us
    gather x1, local copies, waits for them, and re-layouts, chunk_sum(): dense = jnp.take(flat_packed, idx.reshape(-1), axis=0)  4.6 us
    dot_general x1, local copies, waits for them, and re-layouts, chunk_sum(): jnp.einsum('ijab,jbc->iac', dense, rhs, preferred_element_type=jnp.float32)  3.54 us
    dot_general x1, other arithmetic, chunk_sum(): jnp.einsum('ijab,jbc->iac', dense, rhs, preferred_element_type=jnp.float32)  2.56 us
    dot_general x1, matrix products, chunk_sum(): jnp.einsum('ijab,jbc->iac', dense, rhs, preferred_element_type=jnp.float32)  2.27 us
  transfers between devices with their start and end apart: 1, of which 1 were waited for; matrix products, arithmetic and copies ran while one was open for 5% of the time, Pallas kernels for 0%

commit v1 on v0

--- a/solution.py
+++ b/solution.py
@@ -48,7 +48,27 @@
     take_idx = source_row + (jnp.arange(inner_blocks, dtype=jnp.int32) * row_blocks)[:, None]
     packed = jnp.take(flat_blocks, take_idx.reshape(-1), axis=0)
     packed = packed.reshape(inner_blocks, slots, BLK, BLK)
-    gathered = lax.all_gather(packed, ("layer", "col"), axis=0, tiled=True)
+    passed, reached, seen_now = (
+        lax.axis_size(("layer", "col")),
+        lax.axis_index(("layer", "col")),
+        packed.shape[0],
+    )
+    leaves = [(k0, (k0 + 1) % passed) for k0 in range(passed)]
+    arrivals = [(k0, (k0 - 1) % passed) for k0 in range(passed)]
+    gathered = jnp.zeros((*packed.shape[:0], passed * seen_now, *packed.shape[1:]), packed.dtype)
+    lower = next_value = packed
+    gathered = lax.dynamic_update_slice_in_dim(gathered, packed, reached * seen_now, axis=0)
+    res = passed // 2
+    for s in range(1, res + 1):
+        lower = lax.ppermute(lower, axis_name=("layer", "col"), perm=leaves)
+        gathered = lax.dynamic_update_slice_in_dim(
+            gathered, lower, (reached - s) % passed * seen_now, axis=0
+        )
+        if s < passed - res:
+            next_value = lax.ppermute(next_value, axis_name=("layer", "col"), perm=arrivals)
+            gathered = lax.dynamic_update_slice_in_dim(
+                gathered, next_value, (reached + s) % passed * seen_now, axis=0
+            )
     first_inner = (layer_idx * row_count + row_idx) * inner_local
     first_col = col_idx * cols_local
     inner_pos = first_inner + lax.broadcasted_iota(jnp.int32, (inner_local, cols_local), 0)

time: 82.1 us -> 70.5 us (0.86)
  between operations: 13.5 us -> 0.19 us
  waiting for transfers between devices: 36.2 us -> 23.9 us
  starting transfers between devices: 0.01 us -> 10.1 us
  local copies, waits for them, and re-layouts: 10.2 us -> 13 us
  blocking collectives: 12.6 us -> 15.1 us
  other arithmetic: 7.08 us -> 5.65 us
    all_gather x1 -> x0, waiting for transfers between devices: 36.2 us -> none  [per_device(): gathered = lax.all_gather(packed, ('layer', 'col'), axis=0, tiled=True)]
    ppermute x0 -> x7, waiting for transfers between devices: none -> 23.9 us  [the longest x3 17.9 us: per_device(): lax.ppermute(next_value, axis_name=('layer', 'col'), perm=arrivals)]
    ppermute x0 -> x7, starting transfers between devices: none -> 10.1 us  [the longest x4 6.82 us: per_device(): lower = lax.ppermute(lower, axis_name=('layer', 'col'), perm=leaves)]
    dynamic_update_slice x0 -> x7, local copies, waits for them, and re-layouts: none -> 3.11 us  [the longest x4 2.05 us: per_device(): lax.dynamic_update_slice_in_dim(gathered, lower, (reached - s) % passed *...]
    all_gather x1, blocking collectives: 12.6 us -> 15.1 us  [per_device(): lax.all_gather(right_factor, ('layer', 'row'), axis=0, tiled=True)]
    gather x1, local copies, waits for them, and re-layouts: 4.6 us -> 3.02 us  [chunk_sum(): dense = jnp.take(flat_packed, idx.reshape(-1), axis=0)]
    dynamic_update_slice x0 -> x1, other arithmetic: none -> 0.9 us  [per_device(): lax.dynamic_update_slice_in_dim(gathered, packed, reached * seen_now, axi...]
    convert_element_type x1, other arithmetic: 0.93 us -> 0.09 us  [per_device(): (unit - 0.5 * square_term.astype(jnp.float32)).astype(jnp.bfloat16)]
  transfers between devices with their start and end apart: 1 -> 7, of which waited for: 1 -> 3; matrix products, arithmetic and copies ran while one was open for 5% -> 9% of each run, Pallas kernels for 0% -> 0%
where the time goes in v1:
time: 70.5 us; the launch traced here: 70.2 us
  waiting for transfers between devices  23.9 us (34%)
  blocking collectives  15.1 us (21%)
  local copies, waits for them, and re-layouts  13 us (18%)
  starting transfers between devices  10.1 us (14%)
  other arithmetic  5.65 us (8%)
  matrix products  2.27 us (3%)
    ppermute x3, waiting for transfers between devices, per_device(): lax.ppermute(next_value, axis_name=('layer', 'col'), perm=arrivals)  17.9 us
    all_gather x1, blocking collectives, per_device(): lax.all_gather(right_factor, ('layer', 'row'), axis=0, tiled=True)  15.1 us
    ppermute x4, starting transfers between devices, per_device(): lower = lax.ppermute(lower, axis_name=('layer', 'col'), perm=leaves)  6.82 us
    ppermute x4, waiting for transfers between devices, per_device(): lower = lax.ppermute(lower, axis_name=('layer', 'col'), perm=leaves)  6.01 us
    dot_general x1, local copies, waits for them, and re-layouts, chunk_sum(): jnp.einsum('ijab,jbc->iac', dense, rhs, preferred_element_type=jnp.float32)  3.55 us
    ppermute x3, starting transfers between devices, per_device(): lax.ppermute(next_value, axis_name=('layer', 'col'), perm=arrivals)  3.3 us
    gather x1, local copies, waits for them, and re-layouts, chunk_sum(): dense = jnp.take(flat_packed, idx.reshape(-1), axis=0)  3.02 us
    dot_general x1, other arithmetic, chunk_sum(): jnp.einsum('ijab,jbc->iac', dense, rhs, preferred_element_type=jnp.float32)  2.56 us
  transfers between devices with their start and end apart: 7, of which 3 were waited for; matrix products, arithmetic and copies ran while one was open for 9% of the time, Pallas kernels for 0%

profile of v1, /device:TPU:0, one launch (start us, length us, event | category | flops | bytes accessed | tf_op | source)
XLA Modules:
  0.0 70.2 jit_solution(3054694393368315144)
XLA Ops:
  0.0 0.8 %compare_bitcast_fusion = (pred[16]{0:T(512)(128)(4,1)S(1)}, s32[16,1]{0,1:T(1,128)S(1)}) fusion(s32[64,8]{0,1:T(8,128)} %param.6, s32[]{:T(128)S(6)} %select_n.137, s32[]{:T(128)S(6)} %select_n.140), kind=kLoop, calls=%fused_computation.37 | loop fusion | flops 48 | bytes 152 | tf_op jit(solution)/shard_map/gt | solution.py:42
  0.8 0.1 copy.30
  1.0 0.1 add_reduce_fusion
  1.1 0.1 select_reduce_fusion
  1.2 0.6 gather_fusion
  1.8 0.5 broadcast_in_dim.72
  2.4 0.9 %constant_dynamic-update-slice_fusion.7 = (bf16[8,8,128,128]{3,2,1,0:T(8,128)(2,1)S(1)}, bf16[1,8,128,128]{3,2,1,0:T(8,128)(2,1)}) fusion(bf16[8,8,128,128]{3,2,1,0:T(8,128)(2,1)S(1)} %broadcast_in_dim.72, s32[]{:T(128)S(6)} %select_n.140, bf16[8,128,128]{2,1,0:T(8,128)(2,1)S(1)} %gather_fusion, pred[8]{0:T(512)(128)(4,1)S(1)} %compare_and_fusion.1), kind=kLoop, calls=%fused_computation.35 | loop fusion | flops 131072 | bytes 786948 | tf_op jit(solution)/shard_map/dynamic_update_slice | solution.py:60
  3.2 3.0 %collective-permute-start = (bf16[1,8,128,128]{3,2,1,0:T(8,128)(2,1)}, bf16[1,8,128,128]{3,2,1,0:T(8,128)(2,1)}, u32[]{:S(2)}, u32[]{:S(2)}) collective-permute-start(bf16[1,8,128,128]{3,2,1,0:T(8,128)(2,1)} %get-tuple-element.8), channel_id=1, source_target_pairs={{0,1},{1,2},{2,3},{3,16},{16,17},{17,18},{18,19},{19,0},{4,5},{5,6... | collective-permute-start | bytes 786440 | tf_op jit(solution)/shard_map/ppermute | solution.py:63
  6.3 3.0 %collective-permute-start.1 = (bf16[1,8,128,128]{3,2,1,0:T(8,128)(2,1)}, bf16[1,8,128,128]{3,2,1,0:T(8,128)(2,1)S(1)}, u32[]{:S(2)}, u32[]{:S(2)}) collective-permute-start(bf16[1,8,128,128]{3,2,1,0:T(8,128)(2,1)} %get-tuple-element.8), channel_id=1, source_target_pairs={{0,19},{1,0},{2,1},{3,2},{16,3},{17,16},{18,17},{19,18},{4,23},{5,... | collective-permute-start | bytes 786440 | tf_op jit(solution)/shard_map/ppermute | solution.py:68
  9.5 0.8 %dynamic-slice_compare_fusion.1 = pred[16,2]{0,1:T(4,128)(4,1)S(1)} fusion(s32[64,8]{0,1:T(8,128)} %param.7, s32[]{:T(128)S(6)} %select_n.137, s32[]{:T(128)S(6)} %select_n.138), kind=kLoop, calls=%fused_computation.40 | loop fusion | flops 32 | bytes 168 | tf_op jit(solution)/shard_map/gt | solution.py:118
  10.3 0.1 broadcast_bitcast_fusion
  10.4 0.1 min.15
  10.5 0.1 add.203
  10.6 0.1 subtract_convert_fusion
  10.7 6.0 %collective-permute-done = bf16[1,8,128,128]{3,2,1,0:T(8,128)(2,1)} collective-permute-done((bf16[1,8,128,128]{3,2,1,0:T(8,128)(2,1)}, bf16[1,8,128,128]{3,2,1,0:T(8,128)(2,1)}, u32[]{:S(2)}, u32[]{:S(2)}) %collective-permute-start) | collective-permute-done | bytes 262176 | tf_op jit(solution)/shard_map/ppermute | solution.py:63
  16.7 15.1 %all_gather.3 = bf16[1024,256]{1,0:T(8,128)(2,1)S(1)} all-gather(bf16[128,256]{1,0:T(8,128)(2,1)S(1)} %subtract_convert_fusion), channel_id=1, replica_groups=mesh['layer'=2,'row'=4,'col'=4] {'layer','row'}, dimensions={0}, use_global_device_ids=true | all-gather | bytes 589824 | tf_op jit(solution)/shard_map/all_gather | solution.py:78
  31.8 0.3 collective-permute-start.3
  32.2 0.1 copy.29
  32.2 0.1 copy.26
  32.3 0.1 broadcast_in_dim.69
  32.5 1.4 %copy.34 = pred[2048,256]{1,0:T(32,128)(4,1)} copy(pred[2048,256]{0,1:T(32,128)(4,1)S(1)} %bitcast.45) | data formatting | bytes 1048576 | tf_op jit(solution)/shard_map/gt | solution.py:118
  33.9 1.7 %collective-permute-start.4 = (bf16[1,8,128,128]{3,2,1,0:T(8,128)(2,1)}, bf16[1,8,128,128]{3,2,1,0:T(8,128)(2,1)S(1)}, u32[]{:S(2)}, u32[]{:S(2)}) collective-permute-start(bf16[1,8,128,128]{3,2,1,0:T(8,128)(2,1)} %collective-permute-done.2), channel_id=1, source_target_pairs={{0,1},{1,2},{2,3},{3,16},{16,17},{17,18},{18,19},{19,0},{4,5},{5,6... | collective-permute-start | bytes 786440 | tf_op jit(solution)/shard_map/ppermute | solution.py:63
  35.6 1.0 %constant_dynamic-update-slice_fusion.6 = bf16[8,8,128,128]{3,2,1,0:T(8,128)(2,1)S(1)} fusion(bf16[8,8,128,128]{3,2,1,0:T(8,128)(2,1)S(1)} %get-tuple-element.7, bf16[1,8,128,128]{3,2,1,0:T(8,128)(2,1)} %collective-permute-done, s32[]{:T(128)S(6)} %select_n.146), kind=kLoop, calls=%fused_computation.34 | loop fusion | bytes 524292 | tf_op jit(solution)/shard_map/dynamic_update_slice | solution.py:64
  36.7 9.8 %collective-permute-done.3 = bf16[1,8,128,128]{3,2,1,0:T(8,128)(2,1)} collective-permute-done((bf16[1,8,128,128]{3,2,1,0:T(8,128)(2,1)S(1)}, bf16[1,8,128,128]{3,2,1,0:T(8,128)(2,1)}, u32[]{:S(2)}, u32[]{:S(2)}) %collective-permute-start.3) | collective-permute-done | bytes 262176 | tf_op jit(solution)/shard_map/ppermute | solution.py:68
  46.5 1.0 %constant_dynamic-update-slice_fusion.4 = bf16[8,8,128,128]{3,2,1,0:T(8,128)(2,1)S(1)} fusion(bf16[8,8,128,128]{3,2,1,0:T(8,128)(2,1)S(1)} %constant_dynamic-update-slice_fusion.5, bf16[1,8,128,128]{3,2,1,0:T(8,128)(2,1)} %collective-permute-done.2, s32[]{:T(128)S(6)} %select_n.150), kind=kLoop, calls=%fused_computation.32 | loop fusion | bytes 524292 | tf_op jit(solution)/shard_map/dynamic_update_slice | solution.py:64
  47.5 2.1 %collective-permute-start.6 = (bf16[1,8,128,128]{3,2,1,0:T(8,128)(2,1)S(1)}, bf16[1,8,128,128]{3,2,1,0:T(8,128)(2,1)S(1)}, u32[]{:S(2)}, u32[]{:S(2)}) collective-permute-start(bf16[1,8,128,128]{3,2,1,0:T(8,128)(2,1)S(1)} %collective-permute-done.4), channel_id=1, source_target_pairs={{0,1},{1,2},{2,3},{3,16},{16,17},{17,18},{18,19},{19,0},{4,5},{5,6... | collective-permute-start | bytes 786440 | tf_op jit(solution)/shard_map/ppermute | solution.py:63
  49.6 1.0 %constant_dynamic-update-slice_fusion.3 = bf16[8,8,128,128]{3,2,1,0:T(8,128)(2,1)S(1)} fusion(bf16[8,8,128,128]{3,2,1,0:T(8,128)(2,1)S(1)} %constant_dynamic-update-slice_fusion.4, bf16[1,8,128,128]{3,2,1,0:T(8,128)(2,1)} %collective-permute-done.3, s32[]{:T(128)S(6)} %select_n.152), kind=kLoop, calls=%fused_computation.31 | loop fusion | bytes 524292 | tf_op jit(solution)/shard_map/dynamic_update_slice | solution.py:69
  50.6 8.1 %collective-permute-done.5 = bf16[1,8,128,128]{3,2,1,0:T(8,128)(2,1)S(1)} collective-permute-done((bf16[1,8,128,128]{3,2,1,0:T(8,128)(2,1)}, bf16[1,8,128,128]{3,2,1,0:T(8,128)(2,1)S(1)}, u32[]{:S(2)}, u32[]{:S(2)}) %collective-permute-start.5) | collective-permute-done | bytes 262176 | tf_op jit(solution)/shard_map/ppermute | solution.py:68
  58.8 3.0 %gather_fusion.1 = bf16[128,128,128]{2,1,0:T(8,128)(2,1)} fusion(bf16[64,128,128]{2,1,0:T(8,128)(2,1)S(1)} %bitcast.42, s32[1024]{0:T(1024)S(1)} %pad_clamp_fusion), kind=kCustom, calls=%fused_computation.1 | custom fusion | bytes 8389120 | tf_op jit(solution)/shard_map/jit(_take)/gather | solution.py:92
  61.8 2.6 %select_bitcast_fusion = bf16[16,128,128,8]{2,1,3,0:T(8,128)(2,1)S(1)} fusion(bf16[16,8,128,128]{3,2,1,0:T(8,128)(2,1)} %bitcast.43, pred[16,8]{1,0:T(8,128)(4,1)S(1)} %copy.29, pred[16,8]{1,0:T(8,128)(4,1)S(1)} %copy.26), kind=kLoop, calls=%fused_computation.4 | loop fusion | flops 4194304 | bytes 8388864 | tf_op jit(solution)/shard_map/ijab,jbc->iac/dot_general | solution.py:96
  64.4 3.5 %copy.32 = bf16[16,128,128,8]{2,3,1,0:T(8,128)(2,1)S(1)} copy(bf16[16,128,128,8]{2,1,3,0:T(8,128)(2,1)S(1)} %select_bitcast_fusion) | data formatting | bytes 8388608 | tf_op jit(solution)/shard_map/ijab,jbc->iac/dot_general | solution.py:96
  68.0 2.3 %fusion.8 = bf16[2048,256]{1,0:T(8,128)(2,1)} fusion(pred[2048,256]{1,0:T(32,128)(4,1)S(1)} %copy-done.1, bf16[8,128,256]{2,1,0:T(8,128)(2,1)S(1)} %bitcast.46, bf16[2048,128,8]{1,2,0:T(8,128)(2,1)S(1)} %bitcast.44), kind=kOutput, calls=%fused_computation.7 | convolution fusion | flops 1074790400 | bytes 6291456 | tf_op jit(solution)/shard_map/ijab,jbc->iac/dot_general | solution.py:96
  (36 shorter events, 0.6 us)
Async XLA Ops:
  0.0 1.2 %copy-start = (bf16[2048,128]{1,0:T(8,128)(2,1)S(1)}, bf16[2048,128]{1,0:T(8,128)(2,1)}, u32[]{:S(2)}) copy-start(bf16[2048,128]{1,0:T(8,128)(2,1)} %param.4) | copy-start | bytes 1572868
  0.0 9.2 %copy-start.3 = (s32[64,8]{0,1:T(8,128)S(1)}, s32[64,8]{0,1:T(8,128)}, u32[]{:S(2)}) copy-start(s32[64,8]{0,1:T(8,128)} %param.6) | copy-start | bytes 6148
  0.0 10.6 %copy-start.2 = (bf16[128,256]{1,0:T(8,128)(2,1)S(1)}, bf16[128,256]{1,0:T(8,128)(2,1)}, u32[]{:S(2)}) copy-start(bf16[128,256]{1,0:T(8,128)(2,1)} %param.5) | copy-start | bytes 196612
  3.2 13.5 %collective-permute-start = (bf16[1,8,128,128]{3,2,1,0:T(8,128)(2,1)}, bf16[1,8,128,128]{3,2,1,0:T(8,128)(2,1)}, u32[]{:S(2)}, u32[]{:S(2)}) collective-permute-start(bf16[1,8,128,128]{3,2,1,0:T(8,128)(2,1)} %get-tuple-element.8), channel_id=1, source_target_pairs={{0,1},{1,2},{2,3},{3,16},{16,17},{17,18},{18,19},{19,0},{4,5},{5,6... | collective-permute-start | bytes 786440 | tf_op jit(solution)/shard_map/ppermute | solution.py:63
  6.3 25.5 %collective-permute-start.1 = (bf16[1,8,128,128]{3,2,1,0:T(8,128)(2,1)}, bf16[1,8,128,128]{3,2,1,0:T(8,128)(2,1)S(1)}, u32[]{:S(2)}, u32[]{:S(2)}) collective-permute-start(bf16[1,8,128,128]{3,2,1,0:T(8,128)(2,1)} %get-tuple-element.8), channel_id=1, source_target_pairs={{0,19},{1,0},{2,1},{3,2},{16,3},{17,16},{18,17},{19,18},{4,23},{5,... | collective-permute-start | bytes 786440 | tf_op jit(solution)/shard_map/ppermute | solution.py:68
  16.7 17.2 %collective-permute-start.2 = (bf16[1,8,128,128]{3,2,1,0:T(8,128)(2,1)}, bf16[1,8,128,128]{3,2,1,0:T(8,128)(2,1)}, u32[]{:S(2)}, u32[]{:S(2)}) collective-permute-start(bf16[1,8,128,128]{3,2,1,0:T(8,128)(2,1)} %collective-permute-done), channel_id=1, source_target_pairs={{0,1},{1,2},{2,3},{3,16},{16,17},{17,18},{18,19},{19,0},{4,5},{5,6... | collective-permute-start | bytes 786440 | tf_op jit(solution)/shard_map/ppermute | solution.py:63
  31.8 14.7 %collective-permute-start.3 = (bf16[1,8,128,128]{3,2,1,0:T(8,128)(2,1)S(1)}, bf16[1,8,128,128]{3,2,1,0:T(8,128)(2,1)}, u32[]{:S(2)}, u32[]{:S(2)}) collective-permute-start(bf16[1,8,128,128]{3,2,1,0:T(8,128)(2,1)S(1)} %collective-permute-done.1), channel_id=1, source_target_pairs={{0,19},{1,0},{2,1},{3,2},{16,3},{17,16},{18,17},{19,18},{4,23},{5,... | collective-permute-start | bytes 786440 | tf_op jit(solution)/shard_map/ppermute | solution.py:68
  33.9 13.6 %collective-permute-start.4 = (bf16[1,8,128,128]{3,2,1,0:T(8,128)(2,1)}, bf16[1,8,128,128]{3,2,1,0:T(8,128)(2,1)S(1)}, u32[]{:S(2)}, u32[]{:S(2)}) collective-permute-start(bf16[1,8,128,128]{3,2,1,0:T(8,128)(2,1)} %collective-permute-done.2), channel_id=1, source_target_pairs={{0,1},{1,2},{2,3},{3,16},{16,17},{17,18},{18,19},{19,0},{4,5},{5,6... | collective-permute-start | bytes 786440 | tf_op jit(solution)/shard_map/ppermute | solution.py:63
  46.5 12.2 %collective-permute-start.5 = (bf16[1,8,128,128]{3,2,1,0:T(8,128)(2,1)}, bf16[1,8,128,128]{3,2,1,0:T(8,128)(2,1)S(1)}, u32[]{:S(2)}, u32[]{:S(2)}) collective-permute-start(bf16[1,8,128,128]{3,2,1,0:T(8,128)(2,1)} %collective-permute-done.3), channel_id=1, source_target_pairs={{0,19},{1,0},{2,1},{3,2},{16,3},{17,16},{18,17},{19,18},{4,23},{5,... | collective-permute-start | bytes 786440 | tf_op jit(solution)/shard_map/ppermute | solution.py:68
  47.5 11.2 %collective-permute-start.6 = (bf16[1,8,128,128]{3,2,1,0:T(8,128)(2,1)S(1)}, bf16[1,8,128,128]{3,2,1,0:T(8,128)(2,1)S(1)}, u32[]{:S(2)}, u32[]{:S(2)}) collective-permute-start(bf16[1,8,128,128]{3,2,1,0:T(8,128)(2,1)S(1)} %collective-permute-done.4), channel_id=1, source_target_pairs={{0,1},{1,2},{2,3},{3,16},{16,17},{17,18},{18,19},{19,0},{4,5},{5,6... | collective-permute-start | bytes 786440 | tf_op jit(solution)/shard_map/ppermute | solution.py:63
  64.4 3.6 %copy-start.1 = (pred[2048,256]{1,0:T(32,128)(4,1)S(1)}, pred[2048,256]{1,0:T(32,128)(4,1)}, u32[]{:S(2)}) copy-start(pred[2048,256]{1,0:T(32,128)(4,1)} %copy.34) | copy-start | bytes 1572868
